TPU v7x, 32 devices: a whole 2x2x4 slice. The times are simulated.
32 devices in a mesh: req: 4 (over x, core), tok: 8 (over z, y).
Axes of the slice: x: 2, y: 2, z: 4, core: 2. Of those that a mesh axis runs over, the one named last changes fastest.
Arguments:
- queries: bfloat16 [8, 2048, 2048], P('req', 'tok'), may hold values from -16 to 16
- new_kv: bfloat16 [8, 2048, 256], P('req', 'tok'), may hold values from -6 to 6
- cache_kv: bfloat16 [8, 4096, 256], P('req', 'tok'), may hold values from -6 to 6
- residual: bfloat16 [8, 2048, 2048], P('req', 'tok'), may hold values from -24 to 24
- prefix_len: int32 [8], replicated, may hold values from 0 to 4096, as said below
- dest_map: int32 [8, 2048], P('req', 'tok'), may hold values from -1 to 4095, as said below
- w_out: bfloat16 [2048, 2048], replicated, may hold values from -0.125 to 0.125
- b_out: float32 [2048], replicated, may hold values from -4 to 4
- ln_gain: float32 [2048], replicated, may hold values from 0.1 to 1.9
- ln_bias: float32 [2048], replicated, may hold values from -4 to 4
- w_up: bfloat16 [2048, 8192], P(None, 'tok'), may hold values from -0.125 to 0.125
- b_up: float32 [8192], P('tok'), may hold values from -6 to 6
- w_down: bfloat16 [8192, 2048], P('tok'), may hold values from -0.0625 to 0.0625
- b_down: float32 [2048], replicated, may hold values from -4 to 4
Outputs:
- layer_out: bfloat16 [4096, 2048], P(('req', 'tok'))
Inputs may be any that keep to these rules, and one draw needn't show every extreme that they name: `prefix_len`: some request uses all 4096 cached positions. In each request the slots that are not -1 are its first n, with n from 128 to 2048; the n over all requests sum to 4096 and the largest is exactly 2048. These slots hold distinct rows of layer_out, every row held by exactly one of them. The live slots of one device's block of dest_map name at most 16 rows of any one device's block of layer_out.
All inputs are finite; a program needn't handle non-finite values.
Results may differ from a plain program's by a relative error of at most 0.012.
Values may be sent and summed in bfloat16 or wider, within the bound.
No kernel may reach another device: no remote copies, remote signals or barrier semaphores. Data moves between devices by JAX's collectives and lax.ppermute only.
A program may use at most 192 MiB of HBM per device.

v0:
```python
import math
import jax
import jax.numpy as jnp
from jax import lax
from jax.sharding import PartitionSpec as P

TOK_DEV = 128
neg_large = -1e30
ln_eps = 1e-05


def attend_block(
    state, block, block_start, queries_four, query_pos, own_prefix, shard_keys, shard_prefix, scale
):
    running_max, running_sum, accum = state
    count = block.shape[1]
    head_dim = queries_four.shape[-1]
    index_all = block_start + jnp.arange(count, dtype=jnp.int32)
    owner = index_all // shard_keys
    offset = index_all % shard_keys
    in_prefix = offset < shard_prefix
    prefix_pos = owner * shard_prefix + offset
    new_pos = owner * (shard_keys - shard_prefix) + offset - shard_prefix
    prefix_seen = prefix_pos[None, None, :] < own_prefix[:, None, None]
    new_seen = new_pos[None, None, :] <= query_pos[None, :, None]
    visible = jnp.where(in_prefix[None, None, :], prefix_seen, new_seen)[:, None, :, :]
    scores = (
        jnp.einsum(
            "rqhd,rkd->rhqk",
            queries_four,
            block[:, :, :head_dim],
            preferred_element_type=jnp.float32,
        )
        * scale
    )
    scores = jnp.where(visible, scores, neg_large)
    new_max = jnp.maximum(running_max, jnp.max(scores, axis=-1))
    probs = jnp.where(visible, jnp.exp(scores - new_max[..., None]), 0.0)
    factor = jnp.exp(running_max - new_max)
    new_sum = running_sum * factor + jnp.sum(probs, axis=-1)
    update = jnp.einsum(
        "rhqk,rkd->rhqd",
        probs.astype(jnp.bfloat16),
        block[:, :, head_dim:],
        preferred_element_type=jnp.float32,
    )
    return (new_max, new_sum, accum * factor[..., None] + update)


def project_rows(attended, residual_rows, w_out, b_out):
    total = (
        residual_rows.astype(jnp.float32)
        + jnp.dot(attended, w_out, preferred_element_type=jnp.float32)
        + b_out
    )
    return total.astype(jnp.bfloat16)


def per_device(
    queries,
    new_kv,
    cache_kv,
    residual,
    prefix_len,
    dest_map,
    w_out,
    b_out,
    ln_gain,
    ln_bias,
    w_up,
    b_up,
    w_down,
    b_down,
):
    group = lax.axis_index("req")
    member = lax.axis_index("tok")
    n_group = lax.axis_size("req")
    n_member = lax.axis_size("tok")
    devices = n_group * n_member
    req_dev, slot_dev, width = queries.shape
    head_dim = new_kv.shape[2] // 2
    heads = width // head_dim
    prefix_dev = cache_kv.shape[1]
    shard_keys = prefix_dev + slot_dev
    own_prefix = lax.dynamic_slice_in_dim(prefix_len, group * req_dev, req_dev)
    query_pos = member * slot_dev + jnp.arange(slot_dev, dtype=jnp.int32)
    queries_four = queries.reshape(req_dev, slot_dev, heads, head_dim)
    scale = 1.0 / math.sqrt(head_dim)
    local_keys = jnp.concatenate([cache_kv, new_kv], axis=1)

    def attend(state, block, block_start):
        return attend_block(
            state,
            block,
            block_start,
            queries_four,
            query_pos,
            own_prefix,
            shard_keys,
            prefix_dev,
            scale,
        )

    initial = (
        jnp.full((req_dev, heads, slot_dev), neg_large, jnp.float32),
        jnp.zeros((req_dev, heads, slot_dev), jnp.float32),
        jnp.zeros((req_dev, heads, slot_dev, head_dim), jnp.float32),
    )
    state = initial
    piece = lax.all_gather(local_keys, "tok", axis=1, tiled=True)
    count = piece.shape[1]
    number = count // shard_keys
    blocks = jnp.moveaxis(piece.reshape(req_dev, number, shard_keys, piece.shape[2]), 1, 0)

    def one_block(carry, item):
        block, index = item
        return (attend(carry, block, index * shard_keys), None)

    state, unused = lax.scan(one_block, state, (blocks, jnp.arange(number, dtype=jnp.int32)))
    running_max, running_sum, accum = state
    attended = (accum / running_sum[..., None]).astype(jnp.bfloat16)
    slots = req_dev * slot_dev
    attended = jnp.transpose(attended, (0, 2, 1, 3)).reshape(slots, width)
    residual_flat = residual.reshape(slots, width)
    capacity = (slots + devices - 1) // devices
    target = dest_map.reshape(slots)
    is_live = target >= 0
    peer = jnp.where(is_live, target // TOK_DEV, devices)
    onehot = (peer[:, None] == jnp.arange(devices, dtype=jnp.int32)[None, :]).astype(jnp.int32)
    position = jnp.sum((jnp.cumsum(onehot, axis=0) - 1) * onehot, axis=1)
    where_to = jnp.where(is_live, peer * capacity + position, devices * capacity)
    row_ids = (
        jnp.full((devices * capacity,), -1, jnp.int32)
        .at[where_to]
        .set(target % TOK_DEV, mode="drop")
    )
    payload = jnp.stack([attended, residual_flat], axis=1)
    layers = payload.shape[1]
    send_rows = (
        jnp.zeros((devices * capacity, layers, width), jnp.bfloat16)
        .at[where_to]
        .set(payload, mode="drop")
    )
    rows_in, ids_in = (
        lax.all_to_all(
            send_rows.reshape(devices, capacity, layers, width),
            ("req", "tok"),
            split_axis=0,
            concat_axis=0,
            tiled=True,
        ),
        lax.all_to_all(
            row_ids.reshape(devices, capacity),
            ("req", "tok"),
            split_axis=0,
            concat_axis=0,
            tiled=True,
        ),
    )
    rows_in = rows_in.reshape(devices * capacity, layers, width)
    ids_in = ids_in.reshape(devices * capacity)
    landing = jnp.where(ids_in >= 0, ids_in, TOK_DEV)
    even_rows = (
        jnp.zeros((TOK_DEV, layers, width), jnp.bfloat16).at[landing].set(rows_in, mode="drop")
    )
    hidden_state = project_rows(even_rows[:, 0], even_rows[:, 1], w_out, b_out)
    state_f = hidden_state.astype(jnp.float32)
    mean = jnp.mean(state_f, axis=-1, keepdims=True)
    centered = state_f - mean
    variance = jnp.mean(centered * centered, axis=-1, keepdims=True)
    normed = (centered * lax.rsqrt(variance + ln_eps) * ln_gain + ln_bias).astype(jnp.bfloat16)
    units = jax.nn.gelu(
        jnp.dot(
            lax.all_gather(normed, "tok", axis=0, tiled=True),
            w_up,
            preferred_element_type=jnp.float32,
        )
        + b_up,
        approximate=True,
    )
    terms = jnp.dot(units.astype(jnp.bfloat16), w_down, preferred_element_type=jnp.float32)
    summed = lax.psum_scatter(
        terms.astype(jnp.bfloat16), "tok", scatter_dimension=0, tiled=True
    ).astype(jnp.float32)
    return (state_f + summed + b_down).astype(jnp.bfloat16)


def solution(mesh):
    in_specs = (
        P("req", "tok", None),
        P("req", "tok", None),
        P("req", "tok", None),
        P("req", "tok", None),
        P(),
        P("req", "tok"),
        P(),
        P(),
        P(),
        P(),
        P(None, "tok"),
        P("tok"),
        P("tok", None),
        P(),
    )
    out_specs = P(("req", "tok"), None)
    return jax.shard_map(
        per_device, mesh=mesh, in_specs=in_specs, out_specs=out_specs, check_vma=False
    )
```

profile of v0, /device:TPU:0, one launch (start us, length us, event | category | flops | bytes accessed | tf_op | source)
XLA Modules:
  0.0 847.8 jit_solution(4371409342720919751)
XLA Ops:
  6.5 2.2 pad_maximum_fusion.1
  12.5 2.4 scatter_custom_fusion
  15.6 7.4 all-to-all-start
  23.1 2.5 copy.35
  25.6 3.0 copy.37
  28.8 82.8 %all-gather.3.cloned.1.call-done = bf16[2,6144,256]{2,1,0:T(8,128)(2,1)} async-done(((bf16[2,768,256]{2,1,0:T(8,128)(2,1)}), bf16[2,6144,256]{2,1,0:T(8,128)(2,1)}) %all-gather.3.cloned.1.call-update) | async-done | bytes 6291472 | tf_op jit(solution)/shard_map/all_gather | solution.py:110
  111.6 320.0 %while.17 = (s32[]{:T(128)}, f32[2,16,256]{2,1,0:T(8,128)S(1)}, f32[2,16,256]{2,1,0:T(8,128)S(1)}, f32[2,16,256,128]{3,2,1,0:T(8,128)}, s32[8]{0:T(128)S(1)}, /*...) while((s32[]{:T(128)}, f32[2,16,256]{2,1,0:T(8,128)S(1)}, ...), condition=%wide.region_7.8_spmd.clone, body=%wide.region_4.7_spmd.clone.sunk | while | flops 3306812672 | bytes 90852008 | solution.py:119
  115.1 10.2 %fusion.77 = (f32[2,16,256]{2,1,0:T(8,128)S(1)}, f32[2,768,256,16]{2,1,3,0:T(8,128)}) fusion(pred[2,256,768]{1,2,0:T(8,128)(4,1)S(1)} %broadcast_select_fusion.2, bf16[2,256,16,128]{3,1,2,0:T(8,128)(2,1)S(1)} %get-tuple-element.313, bf16[2,768,256]{2,1,0:T(8,128)(2,1)S(1)} %dynamic-slice_bitcast_fusion.2), kind=kOutput, calls=%fused_computation.6.clone.1 | convolution fusion | flops 1629478912 | bytes 28082176 | tf_op jit(solution)/shard_map/while/body/eval_jaxpr/rqhd,rkd->rhqk/dot_general | solution.py:28
  125.3 11.4 %fusion.78 = f32[2,16,256]{2,1,0:T(8,128)S(1)} fusion(f32[2,768,256,16]{2,1,3,0:T(8,128)} %get-tuple-element.279, f32[2,16,256]{2,1,0:T(8,128)S(1)} %select_maximum_fusion.2, pred[2,256,768]{1,2,0:T(8,128)(4,1)S(1)} %broadcast_select_fusion.2), kind=kLoop, calls=%fused_computation.8.clone.1 | loop fusion | flops 31449088 | bytes 25624576 | tf_op jit(solution)/shard_map/while/body/eval_jaxpr/reduce_sum | solution.py:40
  136.8 14.3 %fusion.80 = f32[2,16,256,128]{3,2,1,0:T(8,128)} fusion(f32[2,16,256,128]{3,2,1,0:T(8,128)} %get-tuple-element.297, f32[2,16,256]{2,1,0:T(8,128)S(1)} %get-tuple-element.281, pred[]{:T(512)S(6)} %compare.19, f32[2,768,256,16]{2,1,3,0:T(8,128)} %get-tuple-element.279, f32[2,16,256]{2,1,0:T(8,128)S(1)} %select_maximum_fusion.2, ...), kind=kOutput, calls=%fused_computation.12.clone.1 | convolution fusion | flops 1645215744 | bytes 34406400 | tf_op jit(solution)/shard_map/while/body/eval_jaxpr/rhqk,rkd->rhqd/dot_general | solution.py:41
  154.6 10.2 %fusion.77 = (f32[2,16,256]{2,1,0:T(8,128)S(1)}, f32[2,768,256,16]{2,1,3,0:T(8,128)}) fusion(pred[2,256,768]{1,2,0:T(8,128)(4,1)S(1)} %broadcast_select_fusion.2, bf16[2,256,16,128]{3,1,2,0:T(8,128)(2,1)S(1)} %get-tuple-element.313, bf16[2,768,256]{2,1,0:T(8,128)(2,1)S(1)} %dynamic-slice_bitcast_fusion.2), kind=kOutput, calls=%fused_computation.6.clone.1 | convolution fusion | flops 1629478912 | bytes 28082176 | tf_op jit(solution)/shard_map/while/body/eval_jaxpr/rqhd,rkd->rhqk/dot_general | solution.py:28
  164.8 11.4 %fusion.78 = f32[2,16,256]{2,1,0:T(8,128)S(1)} fusion(f32[2,768,256,16]{2,1,3,0:T(8,128)} %get-tuple-element.279, f32[2,16,256]{2,1,0:T(8,128)S(1)} %select_maximum_fusion.2, pred[2,256,768]{1,2,0:T(8,128)(4,1)S(1)} %broadcast_select_fusion.2), kind=kLoop, calls=%fused_computation.8.clone.1 | loop fusion | flops 31449088 | bytes 25624576 | tf_op jit(solution)/shard_map/while/body/eval_jaxpr/reduce_sum | solution.py:40
  176.3 14.9 %fusion.80 = f32[2,16,256,128]{3,2,1,0:T(8,128)} fusion(f32[2,16,256,128]{3,2,1,0:T(8,128)} %get-tuple-element.297, f32[2,16,256]{2,1,0:T(8,128)S(1)} %get-tuple-element.281, pred[]{:T(512)S(6)} %compare.19, f32[2,768,256,16]{2,1,3,0:T(8,128)} %get-tuple-element.279, f32[2,16,256]{2,1,0:T(8,128)S(1)} %select_maximum_fusion.2, ...), kind=kOutput, calls=%fused_computation.12.clone.1 | convolution fusion | flops 1645215744 | bytes 34406400 | tf_op jit(solution)/shard_map/while/body/eval_jaxpr/rhqk,rkd->rhqd/dot_general | solution.py:41
  194.6 10.2 %fusion.77 = (f32[2,16,256]{2,1,0:T(8,128)S(1)}, f32[2,768,256,16]{2,1,3,0:T(8,128)}) fusion(pred[2,256,768]{1,2,0:T(8,128)(4,1)S(1)} %broadcast_select_fusion.2, bf16[2,256,16,128]{3,1,2,0:T(8,128)(2,1)S(1)} %get-tuple-element.313, bf16[2,768,256]{2,1,0:T(8,128)(2,1)S(1)} %dynamic-slice_bitcast_fusion.2), kind=kOutput, calls=%fused_computation.6.clone.1 | convolution fusion | flops 1629478912 | bytes 28082176 | tf_op jit(solution)/shard_map/while/body/eval_jaxpr/rqhd,rkd->rhqk/dot_general | solution.py:28
  204.9 11.4 %fusion.78 = f32[2,16,256]{2,1,0:T(8,128)S(1)} fusion(f32[2,768,256,16]{2,1,3,0:T(8,128)} %get-tuple-element.279, f32[2,16,256]{2,1,0:T(8,128)S(1)} %select_maximum_fusion.2, pred[2,256,768]{1,2,0:T(8,128)(4,1)S(1)} %broadcast_select_fusion.2), kind=kLoop, calls=%fused_computation.8.clone.1 | loop fusion | flops 31449088 | bytes 25624576 | tf_op jit(solution)/shard_map/while/body/eval_jaxpr/reduce_sum | solution.py:40
  216.3 14.9 %fusion.80 = f32[2,16,256,128]{3,2,1,0:T(8,128)} fusion(f32[2,16,256,128]{3,2,1,0:T(8,128)} %get-tuple-element.297, f32[2,16,256]{2,1,0:T(8,128)S(1)} %get-tuple-element.281, pred[]{:T(512)S(6)} %compare.19, f32[2,768,256,16]{2,1,3,0:T(8,128)} %get-tuple-element.279, f32[2,16,256]{2,1,0:T(8,128)S(1)} %select_maximum_fusion.2, ...), kind=kOutput, calls=%fused_computation.12.clone.1 | convolution fusion | flops 1645215744 | bytes 34406400 | tf_op jit(solution)/shard_map/while/body/eval_jaxpr/rhqk,rkd->rhqd/dot_general | solution.py:41
  234.7 10.2 %fusion.77 = (f32[2,16,256]{2,1,0:T(8,128)S(1)}, f32[2,768,256,16]{2,1,3,0:T(8,128)}) fusion(pred[2,256,768]{1,2,0:T(8,128)(4,1)S(1)} %broadcast_select_fusion.2, bf16[2,256,16,128]{3,1,2,0:T(8,128)(2,1)S(1)} %get-tuple-element.313, bf16[2,768,256]{2,1,0:T(8,128)(2,1)S(1)} %dynamic-slice_bitcast_fusion.2), kind=kOutput, calls=%fused_computation.6.clone.1 | convolution fusion | flops 1629478912 | bytes 28082176 | tf_op jit(solution)/shard_map/while/body/eval_jaxpr/rqhd,rkd->rhqk/dot_general | solution.py:28
  245.0 11.4 %fusion.78 = f32[2,16,256]{2,1,0:T(8,128)S(1)} fusion(f32[2,768,256,16]{2,1,3,0:T(8,128)} %get-tuple-element.279, f32[2,16,256]{2,1,0:T(8,128)S(1)} %select_maximum_fusion.2, pred[2,256,768]{1,2,0:T(8,128)(4,1)S(1)} %broadcast_select_fusion.2), kind=kLoop, calls=%fused_computation.8.clone.1 | loop fusion | flops 31449088 | bytes 25624576 | tf_op jit(solution)/shard_map/while/body/eval_jaxpr/reduce_sum | solution.py:40
  256.4 14.9 %fusion.80 = f32[2,16,256,128]{3,2,1,0:T(8,128)} fusion(f32[2,16,256,128]{3,2,1,0:T(8,128)} %get-tuple-element.297, f32[2,16,256]{2,1,0:T(8,128)S(1)} %get-tuple-element.281, pred[]{:T(512)S(6)} %compare.19, f32[2,768,256,16]{2,1,3,0:T(8,128)} %get-tuple-element.279, f32[2,16,256]{2,1,0:T(8,128)S(1)} %select_maximum_fusion.2, ...), kind=kOutput, calls=%fused_computation.12.clone.1 | convolution fusion | flops 1645215744 | bytes 34406400 | tf_op jit(solution)/shard_map/while/body/eval_jaxpr/rhqk,rkd->rhqd/dot_general | solution.py:41
  274.8 10.2 %fusion.77 = (f32[2,16,256]{2,1,0:T(8,128)S(1)}, f32[2,768,256,16]{2,1,3,0:T(8,128)}) fusion(pred[2,256,768]{1,2,0:T(8,128)(4,1)S(1)} %broadcast_select_fusion.2, bf16[2,256,16,128]{3,1,2,0:T(8,128)(2,1)S(1)} %get-tuple-element.313, bf16[2,768,256]{2,1,0:T(8,128)(2,1)S(1)} %dynamic-slice_bitcast_fusion.2), kind=kOutput, calls=%fused_computation.6.clone.1 | convolution fusion | flops 1629478912 | bytes 28082176 | tf_op jit(solution)/shard_map/while/body/eval_jaxpr/rqhd,rkd->rhqk/dot_general | solution.py:28
  285.1 11.4 %fusion.78 = f32[2,16,256]{2,1,0:T(8,128)S(1)} fusion(f32[2,768,256,16]{2,1,3,0:T(8,128)} %get-tuple-element.279, f32[2,16,256]{2,1,0:T(8,128)S(1)} %select_maximum_fusion.2, pred[2,256,768]{1,2,0:T(8,128)(4,1)S(1)} %broadcast_select_fusion.2), kind=kLoop, calls=%fused_computation.8.clone.1 | loop fusion | flops 31449088 | bytes 25624576 | tf_op jit(solution)/shard_map/while/body/eval_jaxpr/reduce_sum | solution.py:40
  296.5 14.9 %fusion.80 = f32[2,16,256,128]{3,2,1,0:T(8,128)} fusion(f32[2,16,256,128]{3,2,1,0:T(8,128)} %get-tuple-element.297, f32[2,16,256]{2,1,0:T(8,128)S(1)} %get-tuple-element.281, pred[]{:T(512)S(6)} %compare.19, f32[2,768,256,16]{2,1,3,0:T(8,128)} %get-tuple-element.279, f32[2,16,256]{2,1,0:T(8,128)S(1)} %select_maximum_fusion.2, ...), kind=kOutput, calls=%fused_computation.12.clone.1 | convolution fusion | flops 1645215744 | bytes 34406400 | tf_op jit(solution)/shard_map/while/body/eval_jaxpr/rhqk,rkd->rhqd/dot_general | solution.py:41
  314.9 10.2 %fusion.77 = (f32[2,16,256]{2,1,0:T(8,128)S(1)}, f32[2,768,256,16]{2,1,3,0:T(8,128)}) fusion(pred[2,256,768]{1,2,0:T(8,128)(4,1)S(1)} %broadcast_select_fusion.2, bf16[2,256,16,128]{3,1,2,0:T(8,128)(2,1)S(1)} %get-tuple-element.313, bf16[2,768,256]{2,1,0:T(8,128)(2,1)S(1)} %dynamic-slice_bitcast_fusion.2), kind=kOutput, calls=%fused_computation.6.clone.1 | convolution fusion | flops 1629478912 | bytes 28082176 | tf_op jit(solution)/shard_map/while/body/eval_jaxpr/rqhd,rkd->rhqk/dot_general | solution.py:28
  325.1 11.4 %fusion.78 = f32[2,16,256]{2,1,0:T(8,128)S(1)} fusion(f32[2,768,256,16]{2,1,3,0:T(8,128)} %get-tuple-element.279, f32[2,16,256]{2,1,0:T(8,128)S(1)} %select_maximum_fusion.2, pred[2,256,768]{1,2,0:T(8,128)(4,1)S(1)} %broadcast_select_fusion.2), kind=kLoop, calls=%fused_computation.8.clone.1 | loop fusion | flops 31449088 | bytes 25624576 | tf_op jit(solution)/shard_map/while/body/eval_jaxpr/reduce_sum | solution.py:40
  336.6 14.9 %fusion.80 = f32[2,16,256,128]{3,2,1,0:T(8,128)} fusion(f32[2,16,256,128]{3,2,1,0:T(8,128)} %get-tuple-element.297, f32[2,16,256]{2,1,0:T(8,128)S(1)} %get-tuple-element.281, pred[]{:T(512)S(6)} %compare.19, f32[2,768,256,16]{2,1,3,0:T(8,128)} %get-tuple-element.279, f32[2,16,256]{2,1,0:T(8,128)S(1)} %select_maximum_fusion.2, ...), kind=kOutput, calls=%fused_computation.12.clone.1 | convolution fusion | flops 1645215744 | bytes 34406400 | tf_op jit(solution)/shard_map/while/body/eval_jaxpr/rhqk,rkd->rhqd/dot_general | solution.py:41
  355.0 10.2 %fusion.77 = (f32[2,16,256]{2,1,0:T(8,128)S(1)}, f32[2,768,256,16]{2,1,3,0:T(8,128)}) fusion(pred[2,256,768]{1,2,0:T(8,128)(4,1)S(1)} %broadcast_select_fusion.2, bf16[2,256,16,128]{3,1,2,0:T(8,128)(2,1)S(1)} %get-tuple-element.313, bf16[2,768,256]{2,1,0:T(8,128)(2,1)S(1)} %dynamic-slice_bitcast_fusion.2), kind=kOutput, calls=%fused_computation.6.clone.1 | convolution fusion | flops 1629478912 | bytes 28082176 | tf_op jit(solution)/shard_map/while/body/eval_jaxpr/rqhd,rkd->rhqk/dot_general | solution.py:28
  365.2 11.4 %fusion.78 = f32[2,16,256]{2,1,0:T(8,128)S(1)} fusion(f32[2,768,256,16]{2,1,3,0:T(8,128)} %get-tuple-element.279, f32[2,16,256]{2,1,0:T(8,128)S(1)} %select_maximum_fusion.2, pred[2,256,768]{1,2,0:T(8,128)(4,1)S(1)} %broadcast_select_fusion.2), kind=kLoop, calls=%fused_computation.8.clone.1 | loop fusion | flops 31449088 | bytes 25624576 | tf_op jit(solution)/shard_map/while/body/eval_jaxpr/reduce_sum | solution.py:40
  376.7 14.9 %fusion.80 = f32[2,16,256,128]{3,2,1,0:T(8,128)} fusion(f32[2,16,256,128]{3,2,1,0:T(8,128)} %get-tuple-element.297, f32[2,16,256]{2,1,0:T(8,128)S(1)} %get-tuple-element.281, pred[]{:T(512)S(6)} %compare.19, f32[2,768,256,16]{2,1,3,0:T(8,128)} %get-tuple-element.279, f32[2,16,256]{2,1,0:T(8,128)S(1)} %select_maximum_fusion.2, ...), kind=kOutput, calls=%fused_computation.12.clone.1 | convolution fusion | flops 1645215744 | bytes 34406400 | tf_op jit(solution)/shard_map/while/body/eval_jaxpr/rhqk,rkd->rhqd/dot_general | solution.py:41
  395.0 10.2 %fusion.77 = (f32[2,16,256]{2,1,0:T(8,128)S(1)}, f32[2,768,256,16]{2,1,3,0:T(8,128)}) fusion(pred[2,256,768]{1,2,0:T(8,128)(4,1)S(1)} %broadcast_select_fusion.2, bf16[2,256,16,128]{3,1,2,0:T(8,128)(2,1)S(1)} %get-tuple-element.313, bf16[2,768,256]{2,1,0:T(8,128)(2,1)S(1)} %dynamic-slice_bitcast_fusion.2), kind=kOutput, calls=%fused_computation.6.clone.1 | convolution fusion | flops 1629478912 | bytes 28082176 | tf_op jit(solution)/shard_map/while/body/eval_jaxpr/rqhd,rkd->rhqk/dot_general | solution.py:28
  405.3 11.4 %fusion.78 = f32[2,16,256]{2,1,0:T(8,128)S(1)} fusion(f32[2,768,256,16]{2,1,3,0:T(8,128)} %get-tuple-element.279, f32[2,16,256]{2,1,0:T(8,128)S(1)} %select_maximum_fusion.2, pred[2,256,768]{1,2,0:T(8,128)(4,1)S(1)} %broadcast_select_fusion.2), kind=kLoop, calls=%fused_computation.8.clone.1 | loop fusion | flops 31449088 | bytes 25624576 | tf_op jit(solution)/shard_map/while/body/eval_jaxpr/reduce_sum | solution.py:40
  416.7 14.9 %fusion.80 = f32[2,16,256,128]{3,2,1,0:T(8,128)} fusion(f32[2,16,256,128]{3,2,1,0:T(8,128)} %get-tuple-element.297, f32[2,16,256]{2,1,0:T(8,128)S(1)} %get-tuple-element.281, pred[]{:T(512)S(6)} %compare.19, f32[2,768,256,16]{2,1,3,0:T(8,128)} %get-tuple-element.279, f32[2,16,256]{2,1,0:T(8,128)S(1)} %select_maximum_fusion.2, ...), kind=kOutput, calls=%fused_computation.12.clone.1 | convolution fusion | flops 1645215744 | bytes 34406400 | tf_op jit(solution)/shard_map/while/body/eval_jaxpr/rhqk,rkd->rhqd/dot_general | solution.py:41
  431.6 2.9 fusion.39
  434.5 1.4 copy.38
  435.9 2.3 stack_reshape.6
  438.2 2.6 pad_maximum_fusion
  440.8 6.3 copy.39
  447.1 4.1 broadcast_in_dim.112
  451.2 64.2 %scatter_fusion = bf16[512,2,2048]{2,1,0:T(2,128)(2,1)} fusion(bf16[512,2,2048]{2,1,0:T(2,128)(2,1)} %broadcast_in_dim.112, s32[512]{0:T(512)S(1)} %bitcast.107, bf16[512,2,2048]{2,1,0:T(2,128)(2,1)} %copy.39), kind=kCustom, calls=%fused_computation.1 | custom fusion | bytes 12584960 | tf_op jit(solution)/shard_map/scatter | solution.py:142
  515.4 3.6 all-to-all-start.1
  519.5 1.4 reduce.5
  521.0 93.9 %all-to-all-done.1 = bf16[32,16,2,2048]{3,2,1,0:T(2,128)(2,1)} async-done(((bf16[32,16,2,2048]{3,2,1,0:T(2,128)(2,1)}), bf16[32,16,2,2048]{3,2,1,0:T(2,128)(2,1)}, u32[]{:S(2)}, u32[]{:S(2)}) %all-to-all-start.1) | async-done | bytes 4194336 | tf_op jit(solution)/shard_map/all_to_all | solution.py:145
  615.5 43.0 %scatter_fusion.1 = bf16[128,2,2048]{2,1,0:T(2,128)(2,1)S(1)} fusion(bf16[128,2,2048]{2,1,0:T(2,128)(2,1)S(1)} %broadcast_in_dim.106, s32[512]{0:T(512)S(1)} %bitcast.108, bf16[512,2,2048]{2,1,0:T(2,128)(2,1)} %bitcast.11), kind=kCustom, calls=%fused_computation.2 | custom fusion | bytes 12584960 | tf_op jit(solution)/shard_map/scatter | solution.py:164
  658.5 1.5 fusion.60
  660.1 5.5 fusion.61
  667.0 70.8 %all-gather.5.cloned.1.call-done = bf16[1024,2048]{1,0:T(8,128)(2,1)} async-done(((bf16[128,2048]{1,0:T(8,128)(2,1)}), bf16[1024,2048]{1,0:T(8,128)(2,1)}) %all-gather.5.cloned.1.call-update) | async-done | bytes 4194320 | tf_op jit(solution)/shard_map/all_gather | solution.py:174
  737.7 15.3 %convolution_convert_fusion = bf16[1024,2048]{1,0:T(8,128)(2,1)} fusion(bf16[1024,2048]{1,0:T(8,128)(2,1)} %param.28, f32[1024]{0:T(1024)S(1)} %copy-done.7, bf16[1024,2048]{1,0:T(8,128)(2,1)} %all-gather.5.cloned.1.call-done, bf16[2048,1024]{1,0:T(8,128)(2,1)} %param.26), kind=kOutput, calls=%fused_computation.51 | convolution fusion | flops 8602517504 | bytes 16781312 | tf_op jit(solution)/shard_map/dot_general | solution.py:181
  753.0 86.3 %reduce-scatter.2.cloned.1.call-done = bf16[128,2048]{1,0:T(8,128)(2,1)} async-done(((bf16[1024,2048]{1,0:T(8,128)(2,1)}), bf16[128,2048]{1,0:T(8,128)(2,1)}) %reduce-scatter.2.cloned.1.call-update) | async-done | bytes 524304 | tf_op jit(solution)/shard_map/reduce_scatter | solution.py:182
  839.3 2.0 add_convert_fusion
  (139 shorter events, 29.3 us)
Async XLA Ops:
  6.5 16.5 %copy-start = (bf16[2,256,2048]{2,1,0:T(8,128)(2,1)S(1)}, bf16[2,256,2048]{2,1,0:T(8,128)(2,1)}, u32[]{:S(2)}) copy-start(bf16[2,256,2048]{2,1,0:T(8,128)(2,1)} %param.16) | copy-start | bytes 6291460
  6.5 105.1 %all-gather.3.cloned.1.call-start = ((), (), s32[]{:S(2)}) async-start(), calls=%async_computation.3 | async-start | bytes 7077888 | tf_op jit(solution)/shard_map/all_gather | solution.py:110
  12.5 16.2 %copy-start.5 = (s32[512,1]{0,1:T(1,128)}, s32[512,1]{0,1:T(1,128)S(1)}, u32[]{:S(2)}) copy-start(s32[512,1]{0,1:T(1,128)S(1)} %compare_select_fusion.2) | copy-start | bytes 6148
  15.6 499.8 %all-to-all-start = ((s32[32,1,16]{2,1,0:T(1,128)}), s32[32,1,16]{2,1,0:T(1,128)}, u32[]{:S(2)}, u32[]{:S(2)}) async-start(s32[32,1,16]{2,1,0:T(1,128)} %bitcast.3), calls=%async_computation | async-start | bytes 32768 | tf_op jit(solution)/shard_map/all_to_all | solution.py:152
  23.1 5.6 copy-start.8
  447.1 4.1 copy-start.6
  515.4 99.5 %all-to-all-start.1 = ((bf16[32,16,2,2048]{3,2,1,0:T(2,128)(2,1)}), bf16[32,16,2,2048]{3,2,1,0:T(2,128)(2,1)}, u32[]{:S(2)}, u32[]{:S(2)}) async-start(bf16[32,16,2,2048]{3,2,1,0:T(2,128)(2,1)} %bitcast.97), calls=%async_computation.1 | async-start | bytes 8388608 | tf_op jit(solution)/shard_map/all_to_all | solution.py:145
  519.0 218.8 %all-gather.5.cloned.1.call-start = ((), (), s32[]{:S(2)}) async-start(), calls=%async_computation.4 | async-start | bytes 4718592 | tf_op jit(solution)/shard_map/all_gather | solution.py:174
  658.5 1.5 copy-start.1
  660.1 5.8 copy-start.2
  660.1 5.8 copy-start.3
  660.1 77.7 %copy-start.7 = (f32[1024]{0:T(1024)S(1)}, f32[1024]{0:T(1024)}, u32[]{:S(2)}) copy-start(f32[1024]{0:T(1024)} %param.27) | copy-start | bytes 12292
  666.9 172.4 %reduce-scatter.2.cloned.1.call-start = ((), (), s32[]{:S(2)}) async-start(), calls=%async_computation.5 | async-start | bytes 4718592 | tf_op jit(solution)/shard_map/reduce_scatter | solution.py:182
  753.0 86.3 %copy-start.4 = (f32[2048]{0:T(1024)S(1)}, f32[2048]{0:T(1024)}, u32[]{:S(2)}) copy-start(f32[2048]{0:T(1024)} %param.29) | copy-start | bytes 24580
Sparse Core Ops, SparseCore 0:
  9.6 101.9 all-gather.2
  667.0 70.6 all-gather.4
  753.1 86.1 reduce-scatter.1
where the time goes:
time: 851 us; the launch traced here: 848 us
  waiting for transfers between devices  334 us (39%)
  matrix products  221 us (26%)
  local copies, waits for them, and re-layouts  150 us (18%)
  other arithmetic  112 us (13%)
  between operations  13.3 us (2%)
  starting transfers between devices  11.1 us (1%)
    dot_general x8, matrix products, attend_block(): jnp.einsum('rhqk,rkd->rhqd', probs.astype(jnp.bfloat16), block[:, :, head...  119 us
    all_to_all x1, waiting for transfers between devices, per_device(): lax.all_to_all(send_rows.reshape(devices, capacity, layers, width), ('req...  93.9 us
    reduce_sum x8, other arithmetic, attend_block(): new_sum = running_sum * factor + jnp.sum(probs, axis=-1)  91.3 us
    reduce_scatter x1, waiting for transfers between devices, per_device(): lax.psum_scatter(terms.astype(jnp.bfloat16), 'tok', scatter_dimension=0,...  86.3 us
    all_gather x1, waiting for transfers between devices, per_device(): piece = lax.all_gather(local_keys, 'tok', axis=1, tiled=True)  82.8 us
    dot_general x8, matrix products, attend_block(): jnp.einsum('rqhd,rkd->rhqk', queries_four, block[:, :, :head_dim], prefer...  82 us
    all_gather x1, waiting for transfers between devices, per_device(): lax.all_gather(normed, 'tok', axis=0, tiled=True)  70.8 us
    scatter x1, local copies, waits for them, and re-layouts, per_device(): send_rows = jnp.zeros((devices * capacity, layers, width), jnp.bfloat16)....  64.2 us
  transfers between devices with their start and end apart: 5, of which 4 were waited for; matrix products, arithmetic and copies ran while one was open for 49% of the time, Pallas kernels for 0%

commit v1 on v0

--- a/solution.py
+++ b/solution.py
@@ -7,6 +7,19 @@
 TOK_DEV = 128
 neg_large = -1e30
 ln_eps = 1e-05
+
+
+def ring_gather(array, axis, dim):
+    ways = lax.axis_size(axis)
+    up = [(d, (d + 1) % ways) for d in range(ways)]
+    down = [(d, (d - 1) % ways) for d in range(ways)]
+    earlier, later = ([array], [array])
+    for _ in range(ways // 2):
+        earlier.append(lax.ppermute(earlier[-1], axis, up))
+    for _ in range((ways - 1) // 2):
+        later.append(lax.ppermute(later[-1], axis, down))
+    line = jnp.concatenate([*earlier[::-1], *later[1:]], axis=dim)
+    return jnp.roll(line, (lax.axis_index(axis) - ways // 2) * array.shape[dim], axis=dim)
 
 
 def attend_block(
@@ -107,7 +120,7 @@
         jnp.zeros((req_dev, heads, slot_dev, head_dim), jnp.float32),
     )
     state = initial
-    piece = lax.all_gather(local_keys, "tok", axis=1, tiled=True)
+    piece = ring_gather(local_keys, "tok", 1)
     count = piece.shape[1]
     number = count // shard_keys
     blocks = jnp.moveaxis(piece.reshape(req_dev, number, shard_keys, piece.shape[2]), 1, 0)

time: 851 us -> 892 us (1.048)
  starting transfers between devices: 11.1 us -> 41.2 us
  local copies, waits for them, and re-layouts: 150 us -> 172 us
  waiting for transfers between devices: 334 us -> 325 us
    all_gather x1 -> x0, waiting for transfers between devices: 82.8 us -> none  [per_device(): piece = lax.all_gather(local_keys, 'tok', axis=1, tiled=True)]
    ppermute x0 -> x7, waiting for transfers between devices: none -> 74.3 us  [the longest x4 64.1 us: ring_gather(): earlier.append(lax.ppermute(earlier[-1], axis, up))]
    ppermute x0 -> x7, starting transfers between devices: none -> 34.4 us  [the longest x3 26.3 us: ring_gather(): later.append(lax.ppermute(later[-1], axis, down))]
    unnamed x22 -> x48, local copies, waits for them, and re-layouts: 6.97 us -> 23.7 us
  transfers between devices with their start and end apart: 5 -> 11, of which waited for: 4 -> 7; matrix products, arithmetic and copies ran while one was open for 49% -> 48% of each run, Pallas kernels for 0% -> 0%
where the time goes in v1:
time: 892 us; the launch traced here: 889 us
  waiting for transfers between devices  325 us (36%)
  matrix products  221 us (25%)
  local copies, waits for them, and re-layouts  172 us (19%)
  other arithmetic  110 us (12%)
  starting transfers between devices  41.2 us (5%)
  between operations  13.8 us (2%)
    dot_general x8, matrix products, attend_block(): jnp.einsum('rhqk,rkd->rhqd', probs.astype(jnp.bfloat16), block[:, :, head...  119 us
    all_to_all x1, waiting for transfers between devices, per_device(): lax.all_to_all(send_rows.reshape(devices, capacity, layers, width), ('req...  93.9 us
    reduce_sum x8, other arithmetic, attend_block(): new_sum = running_sum * factor + jnp.sum(probs, axis=-1)  91.3 us
    reduce_scatter x1, waiting for transfers between devices, per_device(): lax.psum_scatter(terms.astype(jnp.bfloat16), 'tok', scatter_dimension=0,...  86.3 us
    dot_general x8, matrix products, attend_block(): jnp.einsum('rqhd,rkd->rhqk', queries_four, block[:, :, :head_dim], prefer...  81.9 us
    all_gather x1, waiting for transfers between devices, per_device(): lax.all_gather(normed, 'tok', axis=0, tiled=True)  70.8 us
    scatter x1, local copies, waits for them, and re-layouts, per_device(): send_rows = jnp.zeros((devices * capacity, layers, width), jnp.bfloat16)....  64.2 us
    ppermute x4, waiting for transfers between devices, ring_gather(): earlier.append(lax.ppermute(earlier[-1], axis, up))  64.1 us
  transfers between devices with their start and end apart: 11, of which 7 were waited for; matrix products, arithmetic and copies ran while one was open for 48% of the time, Pallas kernels for 0%

profile of v1, /device:TPU:0, one launch (start us, length us, event | category | flops | bytes accessed | tf_op | source)
XLA Modules:
  0.0 888.7 jit_solution(14206645193799168946)
XLA Ops:
  8.7 3.0 collective-permute-start
  11.8 20.6 %collective-permute-done = bf16[2,768,256]{2,1,0:T(8,128)(2,1)S(1)} collective-permute-done((bf16[2,768,256]{2,1,0:T(8,128)(2,1)S(1)}, bf16[2,768,256]{2,1,0:T(8,128)(2,1)S(1)}, u32[]{:S(2)}, u32[]{:S(2)}) %collective-permute-start) | collective-permute-done | bytes 786464 | tf_op jit(solution)/shard_map/ppermute | solution.py:18
  33.2 4.7 collective-permute-start.4
  38.0 28.7 %collective-permute-done.1 = bf16[2,768,256]{2,1,0:T(8,128)(2,1)S(1)} collective-permute-done((bf16[2,768,256]{2,1,0:T(8,128)(2,1)S(1)}, bf16[2,768,256]{2,1,0:T(8,128)(2,1)S(1)}, u32[]{:S(2)}, u32[]{:S(2)}) %collective-permute-start.1) | collective-permute-done | bytes 786464 | tf_op jit(solution)/shard_map/ppermute | solution.py:18
  69.8 17.1 %collective-permute-start.5 = (bf16[2,768,256]{2,1,0:T(8,128)(2,1)}, bf16[2,768,256]{2,1,0:T(8,128)(2,1)}, u32[]{:S(2)}, u32[]{:S(2)}) collective-permute-start(bf16[2,768,256]{2,1,0:T(8,128)(2,1)} %collective-permute-done.4), channel_id=1, source_target_pairs={{0,7},{1,0},{2,1},{3,2},{4,3},{5,4},{6,5},{7,6},{8,15},{9,8},{10,9... | collective-permute-start | bytes 2359304 | tf_op jit(solution)/shard_map/ppermute | solution.py:20
  86.9 14.8 %collective-permute-done.2 = bf16[2,768,256]{2,1,0:T(8,128)(2,1)} collective-permute-done((bf16[2,768,256]{2,1,0:T(8,128)(2,1)S(1)}, bf16[2,768,256]{2,1,0:T(8,128)(2,1)}, u32[]{:S(2)}, u32[]{:S(2)}) %collective-permute-start.2) | collective-permute-done | bytes 786464 | tf_op jit(solution)/shard_map/ppermute | solution.py:18
  110.4 3.2 all-to-all-start
  113.7 3.9 copy.35
  117.7 3.0 copy.37
  120.8 4.5 collective-permute-start.6
  132.5 10.2 %collective-permute-done.6 = bf16[2,768,256]{2,1,0:T(8,128)(2,1)S(1)} collective-permute-done((bf16[2,768,256]{2,1,0:T(8,128)(2,1)}, bf16[2,768,256]{2,1,0:T(8,128)(2,1)S(1)}, u32[]{:S(2)}, u32[]{:S(2)}) %collective-permute-start.6) | collective-permute-done | bytes 786464 | tf_op jit(solution)/shard_map/ppermute | solution.py:20
  148.9 4.2 constant_dynamic-slice_fusion
  153.1 319.0 %while.17 = (s32[]{:T(128)}, f32[2,16,256]{2,1,0:T(8,128)S(1)}, f32[2,16,256]{2,1,0:T(8,128)S(1)}, f32[2,16,256,128]{3,2,1,0:T(8,128)}, s32[8]{0:T(128)S(1)}, /*...) while((s32[]{:T(128)}, f32[2,16,256]{2,1,0:T(8,128)S(1)}, ...), condition=%wide.region_7.8_spmd.clone, body=%wide.region_4.7_spmd.clone.sunk | while | flops 3306812672 | bytes 90852008 | solution.py:132
  156.5 10.2 %fusion.77 = (f32[2,16,256]{2,1,0:T(8,128)S(1)}, f32[2,768,256,16]{2,1,3,0:T(8,128)}) fusion(pred[2,256,768]{1,2,0:T(8,128)(4,1)S(1)} %broadcast_select_fusion.2, bf16[2,256,16,128]{3,1,2,0:T(8,128)(2,1)S(1)} %get-tuple-element.313, bf16[2,768,256]{2,1,0:T(8,128)(2,1)S(1)} %dynamic-slice_bitcast_fusion.2), kind=kOutput, calls=%fused_computation.6.clone.1 | convolution fusion | flops 1629478912 | bytes 28082176 | tf_op jit(solution)/shard_map/while/body/eval_jaxpr/rqhd,rkd->rhqk/dot_general | solution.py:41
  166.7 11.4 %fusion.78 = f32[2,16,256]{2,1,0:T(8,128)S(1)} fusion(f32[2,768,256,16]{2,1,3,0:T(8,128)} %get-tuple-element.279, f32[2,16,256]{2,1,0:T(8,128)S(1)} %select_maximum_fusion.2, pred[2,256,768]{1,2,0:T(8,128)(4,1)S(1)} %broadcast_select_fusion.2), kind=kLoop, calls=%fused_computation.8.clone.1 | loop fusion | flops 31449088 | bytes 25624576 | tf_op jit(solution)/shard_map/while/body/eval_jaxpr/reduce_sum | solution.py:53
  178.2 14.3 %fusion.80 = f32[2,16,256,128]{3,2,1,0:T(8,128)} fusion(f32[2,16,256,128]{3,2,1,0:T(8,128)} %get-tuple-element.297, f32[2,16,256]{2,1,0:T(8,128)S(1)} %get-tuple-element.281, pred[]{:T(512)S(6)} %compare.19, f32[2,768,256,16]{2,1,3,0:T(8,128)} %get-tuple-element.279, f32[2,16,256]{2,1,0:T(8,128)S(1)} %select_maximum_fusion.2, ...), kind=kOutput, calls=%fused_computation.12.clone.1 | convolution fusion | flops 1645215744 | bytes 34406400 | tf_op jit(solution)/shard_map/while/body/eval_jaxpr/rhqk,rkd->rhqd/dot_general | solution.py:54
  195.9 10.2 %fusion.77 = (f32[2,16,256]{2,1,0:T(8,128)S(1)}, f32[2,768,256,16]{2,1,3,0:T(8,128)}) fusion(pred[2,256,768]{1,2,0:T(8,128)(4,1)S(1)} %broadcast_select_fusion.2, bf16[2,256,16,128]{3,1,2,0:T(8,128)(2,1)S(1)} %get-tuple-element.313, bf16[2,768,256]{2,1,0:T(8,128)(2,1)S(1)} %dynamic-slice_bitcast_fusion.2), kind=kOutput, calls=%fused_computation.6.clone.1 | convolution fusion | flops 1629478912 | bytes 28082176 | tf_op jit(solution)/shard_map/while/body/eval_jaxpr/rqhd,rkd->rhqk/dot_general | solution.py:41
  206.1 11.4 %fusion.78 = f32[2,16,256]{2,1,0:T(8,128)S(1)} fusion(f32[2,768,256,16]{2,1,3,0:T(8,128)} %get-tuple-element.279, f32[2,16,256]{2,1,0:T(8,128)S(1)} %select_maximum_fusion.2, pred[2,256,768]{1,2,0:T(8,128)(4,1)S(1)} %broadcast_select_fusion.2), kind=kLoop, calls=%fused_computation.8.clone.1 | loop fusion | flops 31449088 | bytes 25624576 | tf_op jit(solution)/shard_map/while/body/eval_jaxpr/reduce_sum | solution.py:53
  217.6 14.9 %fusion.80 = f32[2,16,256,128]{3,2,1,0:T(8,128)} fusion(f32[2,16,256,128]{3,2,1,0:T(8,128)} %get-tuple-element.297, f32[2,16,256]{2,1,0:T(8,128)S(1)} %get-tuple-element.281, pred[]{:T(512)S(6)} %compare.19, f32[2,768,256,16]{2,1,3,0:T(8,128)} %get-tuple-element.279, f32[2,16,256]{2,1,0:T(8,128)S(1)} %select_maximum_fusion.2, ...), kind=kOutput, calls=%fused_computation.12.clone.1 | convolution fusion | flops 1645215744 | bytes 34406400 | tf_op jit(solution)/shard_map/while/body/eval_jaxpr/rhqk,rkd->rhqd/dot_general | solution.py:54
  235.8 10.2 %fusion.77 = (f32[2,16,256]{2,1,0:T(8,128)S(1)}, f32[2,768,256,16]{2,1,3,0:T(8,128)}) fusion(pred[2,256,768]{1,2,0:T(8,128)(4,1)S(1)} %broadcast_select_fusion.2, bf16[2,256,16,128]{3,1,2,0:T(8,128)(2,1)S(1)} %get-tuple-element.313, bf16[2,768,256]{2,1,0:T(8,128)(2,1)S(1)} %dynamic-slice_bitcast_fusion.2), kind=kOutput, calls=%fused_computation.6.clone.1 | convolution fusion | flops 1629478912 | bytes 28082176 | tf_op jit(solution)/shard_map/while/body/eval_jaxpr/rqhd,rkd->rhqk/dot_general | solution.py:41
  246.1 11.4 %fusion.78 = f32[2,16,256]{2,1,0:T(8,128)S(1)} fusion(f32[2,768,256,16]{2,1,3,0:T(8,128)} %get-tuple-element.279, f32[2,16,256]{2,1,0:T(8,128)S(1)} %select_maximum_fusion.2, pred[2,256,768]{1,2,0:T(8,128)(4,1)S(1)} %broadcast_select_fusion.2), kind=kLoop, calls=%fused_computation.8.clone.1 | loop fusion | flops 31449088 | bytes 25624576 | tf_op jit(solution)/shard_map/while/body/eval_jaxpr/reduce_sum | solution.py:53
  257.5 14.9 %fusion.80 = f32[2,16,256,128]{3,2,1,0:T(8,128)} fusion(f32[2,16,256,128]{3,2,1,0:T(8,128)} %get-tuple-element.297, f32[2,16,256]{2,1,0:T(8,128)S(1)} %get-tuple-element.281, pred[]{:T(512)S(6)} %compare.19, f32[2,768,256,16]{2,1,3,0:T(8,128)} %get-tuple-element.279, f32[2,16,256]{2,1,0:T(8,128)S(1)} %select_maximum_fusion.2, ...), kind=kOutput, calls=%fused_computation.12.clone.1 | convolution fusion | flops 1645215744 | bytes 34406400 | tf_op jit(solution)/shard_map/while/body/eval_jaxpr/rhqk,rkd->rhqd/dot_general | solution.py:54
  275.8 10.2 %fusion.77 = (f32[2,16,256]{2,1,0:T(8,128)S(1)}, f32[2,768,256,16]{2,1,3,0:T(8,128)}) fusion(pred[2,256,768]{1,2,0:T(8,128)(4,1)S(1)} %broadcast_select_fusion.2, bf16[2,256,16,128]{3,1,2,0:T(8,128)(2,1)S(1)} %get-tuple-element.313, bf16[2,768,256]{2,1,0:T(8,128)(2,1)S(1)} %dynamic-slice_bitcast_fusion.2), kind=kOutput, calls=%fused_computation.6.clone.1 | convolution fusion | flops 1629478912 | bytes 28082176 | tf_op jit(solution)/shard_map/while/body/eval_jaxpr/rqhd,rkd->rhqk/dot_general | solution.py:41
  286.0 11.4 %fusion.78 = f32[2,16,256]{2,1,0:T(8,128)S(1)} fusion(f32[2,768,256,16]{2,1,3,0:T(8,128)} %get-tuple-element.279, f32[2,16,256]{2,1,0:T(8,128)S(1)} %select_maximum_fusion.2, pred[2,256,768]{1,2,0:T(8,128)(4,1)S(1)} %broadcast_select_fusion.2), kind=kLoop, calls=%fused_computation.8.clone.1 | loop fusion | flops 31449088 | bytes 25624576 | tf_op jit(solution)/shard_map/while/body/eval_jaxpr/reduce_sum | solution.py:53
  297.5 14.9 %fusion.80 = f32[2,16,256,128]{3,2,1,0:T(8,128)} fusion(f32[2,16,256,128]{3,2,1,0:T(8,128)} %get-tuple-element.297, f32[2,16,256]{2,1,0:T(8,128)S(1)} %get-tuple-element.281, pred[]{:T(512)S(6)} %compare.19, f32[2,768,256,16]{2,1,3,0:T(8,128)} %get-tuple-element.279, f32[2,16,256]{2,1,0:T(8,128)S(1)} %select_maximum_fusion.2, ...), kind=kOutput, calls=%fused_computation.12.clone.1 | convolution fusion | flops 1645215744 | bytes 34406400 | tf_op jit(solution)/shard_map/while/body/eval_jaxpr/rhqk,rkd->rhqd/dot_general | solution.py:54
  315.7 10.2 %fusion.77 = (f32[2,16,256]{2,1,0:T(8,128)S(1)}, f32[2,768,256,16]{2,1,3,0:T(8,128)}) fusion(pred[2,256,768]{1,2,0:T(8,128)(4,1)S(1)} %broadcast_select_fusion.2, bf16[2,256,16,128]{3,1,2,0:T(8,128)(2,1)S(1)} %get-tuple-element.313, bf16[2,768,256]{2,1,0:T(8,128)(2,1)S(1)} %dynamic-slice_bitcast_fusion.2), kind=kOutput, calls=%fused_computation.6.clone.1 | convolution fusion | flops 1629478912 | bytes 28082176 | tf_op jit(solution)/shard_map/while/body/eval_jaxpr/rqhd,rkd->rhqk/dot_general | solution.py:41
  326.0 11.4 %fusion.78 = f32[2,16,256]{2,1,0:T(8,128)S(1)} fusion(f32[2,768,256,16]{2,1,3,0:T(8,128)} %get-tuple-element.279, f32[2,16,256]{2,1,0:T(8,128)S(1)} %select_maximum_fusion.2, pred[2,256,768]{1,2,0:T(8,128)(4,1)S(1)} %broadcast_select_fusion.2), kind=kLoop, calls=%fused_computation.8.clone.1 | loop fusion | flops 31449088 | bytes 25624576 | tf_op jit(solution)/shard_map/while/body/eval_jaxpr/reduce_sum | solution.py:53
  337.4 14.9 %fusion.80 = f32[2,16,256,128]{3,2,1,0:T(8,128)} fusion(f32[2,16,256,128]{3,2,1,0:T(8,128)} %get-tuple-element.297, f32[2,16,256]{2,1,0:T(8,128)S(1)} %get-tuple-element.281, pred[]{:T(512)S(6)} %compare.19, f32[2,768,256,16]{2,1,3,0:T(8,128)} %get-tuple-element.279, f32[2,16,256]{2,1,0:T(8,128)S(1)} %select_maximum_fusion.2, ...), kind=kOutput, calls=%fused_computation.12.clone.1 | convolution fusion | flops 1645215744 | bytes 34406400 | tf_op jit(solution)/shard_map/while/body/eval_jaxpr/rhqk,rkd->rhqd/dot_general | solution.py:54
  355.7 10.2 %fusion.77 = (f32[2,16,256]{2,1,0:T(8,128)S(1)}, f32[2,768,256,16]{2,1,3,0:T(8,128)}) fusion(pred[2,256,768]{1,2,0:T(8,128)(4,1)S(1)} %broadcast_select_fusion.2, bf16[2,256,16,128]{3,1,2,0:T(8,128)(2,1)S(1)} %get-tuple-element.313, bf16[2,768,256]{2,1,0:T(8,128)(2,1)S(1)} %dynamic-slice_bitcast_fusion.2), kind=kOutput, calls=%fused_computation.6.clone.1 | convolution fusion | flops 1629478912 | bytes 28082176 | tf_op jit(solution)/shard_map/while/body/eval_jaxpr/rqhd,rkd->rhqk/dot_general | solution.py:41
  365.9 11.4 %fusion.78 = f32[2,16,256]{2,1,0:T(8,128)S(1)} fusion(f32[2,768,256,16]{2,1,3,0:T(8,128)} %get-tuple-element.279, f32[2,16,256]{2,1,0:T(8,128)S(1)} %select_maximum_fusion.2, pred[2,256,768]{1,2,0:T(8,128)(4,1)S(1)} %broadcast_select_fusion.2), kind=kLoop, calls=%fused_computation.8.clone.1 | loop fusion | flops 31449088 | bytes 25624576 | tf_op jit(solution)/shard_map/while/body/eval_jaxpr/reduce_sum | solution.py:53
  377.4 14.9 %fusion.80 = f32[2,16,256,128]{3,2,1,0:T(8,128)} fusion(f32[2,16,256,128]{3,2,1,0:T(8,128)} %get-tuple-element.297, f32[2,16,256]{2,1,0:T(8,128)S(1)} %get-tuple-element.281, pred[]{:T(512)S(6)} %compare.19, f32[2,768,256,16]{2,1,3,0:T(8,128)} %get-tuple-element.279, f32[2,16,256]{2,1,0:T(8,128)S(1)} %select_maximum_fusion.2, ...), kind=kOutput, calls=%fused_computation.12.clone.1 | convolution fusion | flops 1645215744 | bytes 34406400 | tf_op jit(solution)/shard_map/while/body/eval_jaxpr/rhqk,rkd->rhqd/dot_general | solution.py:54
  395.6 10.2 %fusion.77 = (f32[2,16,256]{2,1,0:T(8,128)S(1)}, f32[2,768,256,16]{2,1,3,0:T(8,128)}) fusion(pred[2,256,768]{1,2,0:T(8,128)(4,1)S(1)} %broadcast_select_fusion.2, bf16[2,256,16,128]{3,1,2,0:T(8,128)(2,1)S(1)} %get-tuple-element.313, bf16[2,768,256]{2,1,0:T(8,128)(2,1)S(1)} %dynamic-slice_bitcast_fusion.2), kind=kOutput, calls=%fused_computation.6.clone.1 | convolution fusion | flops 1629478912 | bytes 28082176 | tf_op jit(solution)/shard_map/while/body/eval_jaxpr/rqhd,rkd->rhqk/dot_general | solution.py:41
  405.9 11.4 %fusion.78 = f32[2,16,256]{2,1,0:T(8,128)S(1)} fusion(f32[2,768,256,16]{2,1,3,0:T(8,128)} %get-tuple-element.279, f32[2,16,256]{2,1,0:T(8,128)S(1)} %select_maximum_fusion.2, pred[2,256,768]{1,2,0:T(8,128)(4,1)S(1)} %broadcast_select_fusion.2), kind=kLoop, calls=%fused_computation.8.clone.1 | loop fusion | flops 31449088 | bytes 25624576 | tf_op jit(solution)/shard_map/while/body/eval_jaxpr/reduce_sum | solution.py:53
  417.3 14.9 %fusion.80 = f32[2,16,256,128]{3,2,1,0:T(8,128)} fusion(f32[2,16,256,128]{3,2,1,0:T(8,128)} %get-tuple-element.297, f32[2,16,256]{2,1,0:T(8,128)S(1)} %get-tuple-element.281, pred[]{:T(512)S(6)} %compare.19, f32[2,768,256,16]{2,1,3,0:T(8,128)} %get-tuple-element.279, f32[2,16,256]{2,1,0:T(8,128)S(1)} %select_maximum_fusion.2, ...), kind=kOutput, calls=%fused_computation.12.clone.1 | convolution fusion | flops 1645215744 | bytes 34406400 | tf_op jit(solution)/shard_map/while/body/eval_jaxpr/rhqk,rkd->rhqd/dot_general | solution.py:54
  435.6 10.2 %fusion.77 = (f32[2,16,256]{2,1,0:T(8,128)S(1)}, f32[2,768,256,16]{2,1,3,0:T(8,128)}) fusion(pred[2,256,768]{1,2,0:T(8,128)(4,1)S(1)} %broadcast_select_fusion.2, bf16[2,256,16,128]{3,1,2,0:T(8,128)(2,1)S(1)} %get-tuple-element.313, bf16[2,768,256]{2,1,0:T(8,128)(2,1)S(1)} %dynamic-slice_bitcast_fusion.2), kind=kOutput, calls=%fused_computation.6.clone.1 | convolution fusion | flops 1629478912 | bytes 28082176 | tf_op jit(solution)/shard_map/while/body/eval_jaxpr/rqhd,rkd->rhqk/dot_general | solution.py:41
  445.8 11.4 %fusion.78 = f32[2,16,256]{2,1,0:T(8,128)S(1)} fusion(f32[2,768,256,16]{2,1,3,0:T(8,128)} %get-tuple-element.279, f32[2,16,256]{2,1,0:T(8,128)S(1)} %select_maximum_fusion.2, pred[2,256,768]{1,2,0:T(8,128)(4,1)S(1)} %broadcast_select_fusion.2), kind=kLoop, calls=%fused_computation.8.clone.1 | loop fusion | flops 31449088 | bytes 25624576 | tf_op jit(solution)/shard_map/while/body/eval_jaxpr/reduce_sum | solution.py:53
  457.3 14.9 %fusion.80 = f32[2,16,256,128]{3,2,1,0:T(8,128)} fusion(f32[2,16,256,128]{3,2,1,0:T(8,128)} %get-tuple-element.297, f32[2,16,256]{2,1,0:T(8,128)S(1)} %get-tuple-element.281, pred[]{:T(512)S(6)} %compare.19, f32[2,768,256,16]{2,1,3,0:T(8,128)} %get-tuple-element.279, f32[2,16,256]{2,1,0:T(8,128)S(1)} %select_maximum_fusion.2, ...), kind=kOutput, calls=%fused_computation.12.clone.1 | convolution fusion | flops 1645215744 | bytes 34406400 | tf_op jit(solution)/shard_map/while/body/eval_jaxpr/rhqk,rkd->rhqd/dot_general | solution.py:54
  472.2 2.9 fusion.39
  481.3 6.3 copy.39
  487.6 4.1 broadcast_in_dim.112
  491.7 64.2 %scatter_fusion = bf16[512,2,2048]{2,1,0:T(2,128)(2,1)} fusion(bf16[512,2,2048]{2,1,0:T(2,128)(2,1)} %broadcast_in_dim.112, s32[512]{0:T(512)S(1)} %bitcast.107, bf16[512,2,2048]{2,1,0:T(2,128)(2,1)} %copy.39), kind=kCustom, calls=%fused_computation.1 | custom fusion | bytes 12584960 | tf_op jit(solution)/shard_map/scatter | solution.py:155
  555.9 3.6 all-to-all-start.1
  561.6 93.9 %all-to-all-done.1 = bf16[32,16,2,2048]{3,2,1,0:T(2,128)(2,1)} async-done(((bf16[32,16,2,2048]{3,2,1,0:T(2,128)(2,1)}), bf16[32,16,2,2048]{3,2,1,0:T(2,128)(2,1)}, u32[]{:S(2)}, u32[]{:S(2)}) %all-to-all-start.1) | async-done | bytes 4194336 | tf_op jit(solution)/shard_map/all_to_all | solution.py:158
  656.0 43.0 %scatter_fusion.1 = bf16[128,2,2048]{2,1,0:T(2,128)(2,1)S(1)} fusion(bf16[128,2,2048]{2,1,0:T(2,128)(2,1)S(1)} %broadcast_in_dim.106, s32[512]{0:T(512)S(1)} %bitcast.108, bf16[512,2,2048]{2,1,0:T(2,128)(2,1)} %bitcast.11), kind=kCustom, calls=%fused_computation.2 | custom fusion | bytes 12584960 | tf_op jit(solution)/shard_map/scatter | solution.py:177
  700.6 5.5 fusion.61
  707.5 70.8 %all-gather.2.cloned.1.call-done = bf16[1024,2048]{1,0:T(8,128)(2,1)} async-done(((bf16[128,2048]{1,0:T(8,128)(2,1)}), bf16[1024,2048]{1,0:T(8,128)(2,1)}) %all-gather.2.cloned.1.call-update) | async-done | bytes 4194320 | tf_op jit(solution)/shard_map/all_gather | solution.py:187
  778.2 15.3 %convolution_convert_fusion = bf16[1024,2048]{1,0:T(8,128)(2,1)} fusion(bf16[1024,2048]{1,0:T(8,128)(2,1)} %param.28, f32[1024]{0:T(1024)S(1)} %copy-done.11, bf16[1024,2048]{1,0:T(8,128)(2,1)} %all-gather.2.cloned.1.call-done, bf16[2048,1024]{1,0:T(8,128)(2,1)} %param.26), kind=kOutput, calls=%fused_computation.51 | convolution fusion | flops 8602517504 | bytes 16781312 | tf_op jit(solution)/shard_map/dot_general | solution.py:194
  793.5 86.3 %reduce-scatter.2.cloned.1.call-done = bf16[128,2048]{1,0:T(8,128)(2,1)} async-done(((bf16[1024,2048]{1,0:T(8,128)(2,1)}), bf16[128,2048]{1,0:T(8,128)(2,1)}) %reduce-scatter.2.cloned.1.call-update) | async-done | bytes 524304 | tf_op jit(solution)/shard_map/reduce_scatter | solution.py:195
  (178 shorter events, 63.9 us)
Async XLA Ops:
  6.5 123.5 %copy-start = (bf16[2,512,256]{2,1,0:T(8,128)(2,1)S(1)}, bf16[2,512,256]{2,1,0:T(8,128)(2,1)}, u32[]{:S(2)}) copy-start(bf16[2,512,256]{2,1,0:T(8,128)(2,1)} %param.18) | copy-start | bytes 1572868
  6.5 114.2 %copy-start.12 = (s32[8]{0:T(128)S(1)}, s32[8]{0:T(128)}, u32[]{:S(2)}) copy-start(s32[8]{0:T(128)} %param.20) | copy-start | bytes 100
  7.7 122.4 %copy-start.4 = (bf16[2,256,256]{2,1,0:T(8,128)(2,1)S(1)}, bf16[2,256,256]{2,1,0:T(8,128)(2,1)}, u32[]{:S(2)}) copy-start(bf16[2,256,256]{2,1,0:T(8,128)(2,1)} %param.17) | copy-start | bytes 786436
  8.7 23.6 %collective-permute-start = (bf16[2,768,256]{2,1,0:T(8,128)(2,1)S(1)}, bf16[2,768,256]{2,1,0:T(8,128)(2,1)S(1)}, u32[]{:S(2)}, u32[]{:S(2)}) collective-permute-start(bf16[2,768,256]{2,1,0:T(8,128)(2,1)S(1)} %constant_dynamic-update-slice_fusion), channel_id=1, source_target_pairs={{0,1},{1,2},{2,3},{3,4},{4,5},{5,6},{6,7},{7,0},{8,9},{9,10},{10,1... | collective-permute-start | bytes 2359304 | tf_op jit(solution)/shard_map/ppermute | solution.py:18
  32.3 0.9 copy-start.1
  33.2 33.4 %collective-permute-start.1 = (bf16[2,768,256]{2,1,0:T(8,128)(2,1)S(1)}, bf16[2,768,256]{2,1,0:T(8,128)(2,1)S(1)}, u32[]{:S(2)}, u32[]{:S(2)}) collective-permute-start(bf16[2,768,256]{2,1,0:T(8,128)(2,1)S(1)} %collective-permute-done), channel_id=1, source_target_pairs={{0,1},{1,2},{2,3},{3,4},{4,5},{5,6},{6,7},{7,0},{8,9},{9,10},{10,1... | collective-permute-start | bytes 2359304 | tf_op jit(solution)/shard_map/ppermute | solution.py:18
  33.2 36.6 %collective-permute-start.4 = (bf16[2,768,256]{2,1,0:T(8,128)(2,1)S(1)}, bf16[2,768,256]{2,1,0:T(8,128)(2,1)}, u32[]{:S(2)}, u32[]{:S(2)}) collective-permute-start(bf16[2,768,256]{2,1,0:T(8,128)(2,1)S(1)} %constant_dynamic-update-slice_fusion), channel_id=1, source_target_pairs={{0,7},{1,0},{2,1},{3,2},{4,3},{5,4},{6,5},{7,6},{8,15},{9,8},{10,9... | collective-permute-start | bytes 2359304 | tf_op jit(solution)/shard_map/ppermute | solution.py:20
  66.6 51.0 %copy-start.3 = (bf16[2,768,256]{2,1,0:T(8,128)(2,1)}, bf16[2,768,256]{2,1,0:T(8,128)(2,1)S(1)}, u32[]{:S(2)}) copy-start(bf16[2,768,256]{2,1,0:T(8,128)(2,1)S(1)} %collective-permute-done.1) | copy-start | bytes 2359300
  66.6 35.1 %collective-permute-start.2 = (bf16[2,768,256]{2,1,0:T(8,128)(2,1)S(1)}, bf16[2,768,256]{2,1,0:T(8,128)(2,1)}, u32[]{:S(2)}, u32[]{:S(2)}) collective-permute-start(bf16[2,768,256]{2,1,0:T(8,128)(2,1)S(1)} %collective-permute-done.1), channel_id=1, source_target_pairs={{0,1},{1,2},{2,3},{3,4},{4,5},{5,6},{6,7},{7,0},{8,9},{9,10},{10,1... | collective-permute-start | bytes 2359304 | tf_op jit(solution)/shard_map/ppermute | solution.py:18
  69.8 51.0 %collective-permute-start.5 = (bf16[2,768,256]{2,1,0:T(8,128)(2,1)}, bf16[2,768,256]{2,1,0:T(8,128)(2,1)}, u32[]{:S(2)}, u32[]{:S(2)}) collective-permute-start(bf16[2,768,256]{2,1,0:T(8,128)(2,1)} %collective-permute-done.4), channel_id=1, source_target_pairs={{0,7},{1,0},{2,1},{3,2},{4,3},{5,4},{6,5},{7,6},{8,15},{9,8},{10,9... | collective-permute-start | bytes 2359304 | tf_op jit(solution)/shard_map/ppermute | solution.py:20
  101.8 23.6 %collective-permute-start.3 = (bf16[2,768,256]{2,1,0:T(8,128)(2,1)}, bf16[2,768,256]{2,1,0:T(8,128)(2,1)}, u32[]{:S(2)}, u32[]{:S(2)}) collective-permute-start(bf16[2,768,256]{2,1,0:T(8,128)(2,1)} %collective-permute-done.2), channel_id=1, source_target_pairs={{0,1},{1,2},{2,3},{3,4},{4,5},{5,6},{6,7},{7,0},{8,9},{9,10},{10,1... | collective-permute-start | bytes 2359304 | tf_op jit(solution)/shard_map/ppermute | solution.py:18
  107.3 10.4 %copy-start.9 = (s32[512,1]{0,1:T(1,128)}, s32[512,1]{0,1:T(1,128)S(1)}, u32[]{:S(2)}) copy-start(s32[512,1]{0,1:T(1,128)S(1)} %compare_select_fusion.2) | copy-start | bytes 6148
  110.4 445.5 %all-to-all-start = ((s32[32,1,16]{2,1,0:T(1,128)}), s32[32,1,16]{2,1,0:T(1,128)}, u32[]{:S(2)}, u32[]{:S(2)}) async-start(s32[32,1,16]{2,1,0:T(1,128)} %bitcast.3), calls=%async_computation | async-start | bytes 32768 | tf_op jit(solution)/shard_map/all_to_all | solution.py:165
  120.8 25.5 %copy-start.2 = (bf16[2,768,256]{2,1,0:T(8,128)(2,1)S(1)}, bf16[2,768,256]{2,1,0:T(8,128)(2,1)}, u32[]{:S(2)}) copy-start(bf16[2,768,256]{2,1,0:T(8,128)(2,1)} %copy-done.1) | copy-start | bytes 2359300
  120.8 21.9 %collective-permute-start.6 = (bf16[2,768,256]{2,1,0:T(8,128)(2,1)}, bf16[2,768,256]{2,1,0:T(8,128)(2,1)S(1)}, u32[]{:S(2)}, u32[]{:S(2)}) collective-permute-start(bf16[2,768,256]{2,1,0:T(8,128)(2,1)} %collective-permute-done.5), channel_id=1, source_target_pairs={{0,7},{1,0},{2,1},{3,2},{4,3},{5,4},{6,5},{7,6},{8,15},{9,8},{10,9... | collective-permute-start | bytes 2359304 | tf_op jit(solution)/shard_map/ppermute | solution.py:20
  481.3 10.4 %copy-start.10 = (s32[512,1]{0,1:T(1,128)S(1)}, s32[512,1]{0,1:T(1,128)}, u32[]{:S(2)}) copy-start(s32[512,1]{0,1:T(1,128)} %copy-done.9) | copy-start | bytes 6148
  555.9 99.5 %all-to-all-start.1 = ((bf16[32,16,2,2048]{3,2,1,0:T(2,128)(2,1)}), bf16[32,16,2,2048]{3,2,1,0:T(2,128)(2,1)}, u32[]{:S(2)}, u32[]{:S(2)}) async-start(bf16[32,16,2,2048]{3,2,1,0:T(2,128)(2,1)} %bitcast.97), calls=%async_computation.1 | async-start | bytes 8388608 | tf_op jit(solution)/shard_map/all_to_all | solution.py:158
  559.5 218.7 %all-gather.2.cloned.1.call-start = ((), (), s32[]{:S(2)}) async-start(), calls=%async_computation.3 | async-start | bytes 4718592 | tf_op jit(solution)/shard_map/all_gather | solution.py:187
  656.0 44.6 %copy-start.5 = (f32[2048]{0:T(1024)S(1)}, f32[2048]{0:T(1024)}, u32[]{:S(2)}) copy-start(f32[2048]{0:T(1024)} %param.23) | copy-start | bytes 24580
  700.6 5.8 copy-start.6
  700.6 5.8 copy-start.7
  700.6 77.7 %copy-start.11 = (f32[1024]{0:T(1024)S(1)}, f32[1024]{0:T(1024)}, u32[]{:S(2)}) copy-start(f32[1024]{0:T(1024)} %param.27) | copy-start | bytes 12292
  707.4 172.4 %copy-start.8 = (f32[2048]{0:T(1024)S(1)}, f32[2048]{0:T(1024)}, u32[]{:S(2)}) copy-start(f32[2048]{0:T(1024)} %param.29) | copy-start | bytes 24580
  707.4 172.4 %reduce-scatter.2.cloned.1.call-start = ((), (), s32[]{:S(2)}) async-start(), calls=%async_computation.4 | async-start | bytes 4718592 | tf_op jit(solution)/shard_map/reduce_scatter | solution.py:195
Sparse Core Ops, SparseCore 0:
  707.5 70.6 all-gather.1
  793.6 86.1 reduce-scatter.1
